TPU v7x, 256 devices: a whole 4x4x8 slice. The times are simulated.
256 devices in a mesh: dp: 8 (over x, core), seq: 32 (over y, z).
Axes of the slice: x: 4, y: 4, z: 8, core: 2. Of those that a mesh axis runs over, the one named last changes fastest.
Arguments:
- activations: bfloat16 [8, 4096, 2048], P('dp', 'seq'), may hold values from -16 to 16
- w_query: bfloat16 [2048, 2048], P('seq')
- w_key: bfloat16 [2048, 256], P('seq')
- w_value: bfloat16 [2048, 256], P('seq'), may hold values from -0.125 to 0.125
- key_blocks: int32 [32, 32, 7], replicated, may hold values from 0 to 31, as said below
- random_count: int32 [32], replicated, may hold values from 1 to 3, 64 in all
- grad_out: bfloat16 [8, 4096, 2048], P('dp', 'seq'), may hold values from -6 to 6
Outputs:
- attn_out: bfloat16 [8, 4096, 2048], P('dp', 'seq')
- grad_x: bfloat16 [8, 4096, 2048], P('dp', 'seq')
- grad_wq: bfloat16 [2048, 2048], P('seq')
- grad_wk: bfloat16 [2048, 256], P('seq')
- grad_wv: bfloat16 [2048, 256], P('seq')
Inputs may be any that keep to these rules, and one draw needn't show every extreme that they name: `key_blocks`: row b of head h: columns 0 to 2 are b - 1, b and b + 1 modulo 32; column 3 is one block of the head, the same in all its rows; columns 4 to 6 are three blocks that differ from each other and from the row's first four entries. Head h uses the first random_count[h] of its three random key blocks; the counts sum to 64.
All inputs are finite; a program needn't handle non-finite values.
Results may differ from a plain program's by a relative error of at most 0.025.
The roundings to bfloat16 on the way count: a program that leaves them out, or rounds other values in their place, can miss the bound.
Values may be sent and summed in bfloat16 or wider, within the bound.
No kernel may reach another device: no remote copies, remote signals or barrier semaphores. Data moves between devices by JAX's collectives and lax.ppermute only.
A program may use at most 128 MiB of HBM per device.

v0:
```python
import math
import jax
import jax.numpy as jnp
from jax import lax
from jax.sharding import PartitionSpec as P

HD = 64
GROUP = 8
masked_score = -1e30
query_group = 4


def head_pass(queries, key_rows, value_rows, grad_head, blocks, extra_count):
    seq_len, head_width = queries.shape
    block_count, slot_count = blocks.shape
    block_len = seq_len // block_count
    score_scale = head_width ** (-0.5)
    key_tiles = key_rows.reshape(block_count, block_len, head_width)
    value_tiles = value_rows.reshape(block_count, block_len, head_width)
    usable = jnp.repeat(jnp.arange(slot_count) < 4 + extra_count, block_len)
    rounds = block_count // query_group
    query_steps = queries.reshape(rounds, query_group, block_len, head_width)
    grad_steps = grad_head.reshape(rounds, query_group, block_len, head_width)
    block_steps = blocks.reshape(rounds, query_group, slot_count)

    def one_step(running, inputs):
        q_part, g_part, chosen = inputs
        k_part = key_tiles[chosen].reshape(query_group, slot_count * block_len, head_width)
        v_part = value_tiles[chosen].reshape(query_group, slot_count * block_len, head_width)
        scores = (
            jnp.einsum("gqe,gke->gqk", q_part, k_part, preferred_element_type=jnp.float32)
            * score_scale
        )
        scores = jnp.where(usable, scores, masked_score)
        highest = jnp.max(scores, axis=-1, keepdims=True)
        exponent = jnp.exp(scores - highest)
        shares = exponent / jnp.sum(exponent, axis=-1, keepdims=True)
        shares_low = shares.astype(jnp.bfloat16)
        attended = jnp.einsum(
            "gqk,gke->gqe", shares_low, v_part, preferred_element_type=jnp.float32
        ).astype(jnp.bfloat16)
        grad_shares = jnp.einsum("gqe,gke->gqk", g_part, v_part, preferred_element_type=jnp.float32)
        weighted = jnp.sum(grad_shares * shares, axis=-1, keepdims=True)
        grad_scores = (shares * (grad_shares - weighted)).astype(jnp.bfloat16)
        grad_query = (
            jnp.einsum("gqk,gke->gqe", grad_scores, k_part, preferred_element_type=jnp.float32)
            * score_scale
        ).astype(jnp.bfloat16)
        grad_keys = (
            jnp.einsum("gqk,gqe->gke", grad_scores, q_part, preferred_element_type=jnp.float32)
            * score_scale
        )
        grad_values = jnp.einsum(
            "gqk,gqe->gke", shares_low, g_part, preferred_element_type=jnp.float32
        )
        pieces = jnp.concatenate([grad_keys, grad_values], axis=-1).reshape(
            query_group * slot_count, block_len, 2 * head_width
        )
        running = running.at[chosen.reshape(-1)].add(pieces)
        return (running, (attended, grad_query))

    initial = jnp.zeros((block_count, block_len, 2 * head_width), jnp.float32)
    summed, (attended, grad_query) = lax.scan(
        one_step, initial, (query_steps, grad_steps, block_steps)
    )
    return (
        attended.reshape(seq_len, head_width),
        grad_query.reshape(seq_len, head_width),
        summed.reshape(seq_len, 2 * head_width),
    )


def per_device(activations, w_query, w_key, w_value, key_blocks, random_count, grad_out):
    seq_devices = lax.axis_size("seq")
    dp_devices = lax.axis_size("dp")
    position = lax.axis_index("seq")
    dp_index = lax.axis_index("dp")
    tokens = activations[0]
    grad_rows = grad_out[0]
    tok_count = tokens.shape[0]
    heads = w_query.shape[1] // HD
    kv_heads = w_key.shape[1] // HD
    query_cols = heads * HD
    kv_cols = kv_heads * HD
    all_cols = query_cols + 2 * kv_cols
    w_local = jnp.concatenate([w_query, w_key, w_value], axis=1)
    w_full = lax.all_gather(w_local, "seq", axis=0, tiled=True)
    projected = jnp.dot(tokens, w_full, preferred_element_type=jnp.float32).astype(jnp.bfloat16)
    queries = projected[:, :query_cols]
    key_proj = projected[:, query_cols : query_cols + kv_cols]
    value_proj = projected[:, query_cols + kv_cols :]
    query_pieces = queries.reshape(tok_count, heads, HD).transpose(1, 0, 2)
    grad_pieces = grad_rows.reshape(tok_count, heads, HD).transpose(1, 0, 2)
    paired = jnp.concatenate(
        [key_proj.reshape(tok_count, kv_heads, HD), value_proj.reshape(tok_count, kv_heads, HD)],
        axis=2,
    )
    kv_pieces = jnp.repeat(paired.transpose(1, 0, 2), GROUP, axis=0)
    sent = jnp.concatenate([query_pieces, grad_pieces, kv_pieces], axis=2)
    landed = lax.all_to_all(sent, "seq", split_axis=0, concat_axis=1, tiled=True)[0]
    head_q = landed[:, :HD]
    head_grad = landed[:, HD : 2 * HD]
    head_k = landed[:, 2 * HD : 3 * HD]
    head_v = landed[:, 3 * HD :]
    blocks_mine = lax.dynamic_index_in_dim(key_blocks, position, 0, keepdims=False)
    count_mine = lax.dynamic_index_in_dim(random_count, position, 0, keepdims=False)
    attended, grad_query, grad_kv = head_pass(
        head_q, head_k, head_v, head_grad, blocks_mine, count_mine
    )
    back_sent = jnp.concatenate(
        [
            attended.reshape(seq_devices, tok_count, HD),
            grad_query.reshape(seq_devices, tok_count, HD),
            grad_kv.astype(jnp.bfloat16).reshape(seq_devices, tok_count, 2 * HD),
        ],
        axis=2,
    )
    back = lax.all_to_all(back_sent, "seq", split_axis=0, concat_axis=0, tiled=True)
    back_out = back[:, :, :HD]
    back_query = back[:, :, HD : 2 * HD]
    back_kv = back[:, :, 2 * HD :]
    out_rows = back_out.transpose(1, 0, 2).reshape(tok_count, heads * HD)
    grad_q_rows = back_query.transpose(1, 0, 2).reshape(tok_count, heads * HD)
    kv_sum = jnp.sum(
        back_kv.reshape(kv_heads, GROUP, tok_count, 2 * HD), axis=1, dtype=jnp.float32
    ).astype(jnp.bfloat16)
    grad_k_rows = kv_sum[:, :, :HD].transpose(1, 0, 2).reshape(tok_count, kv_heads * HD)
    grad_v_rows = kv_sum[:, :, HD:].transpose(1, 0, 2).reshape(tok_count, kv_heads * HD)
    combined = jnp.concatenate([grad_q_rows, grad_k_rows, grad_v_rows], axis=1)
    contract = (((1,), (1,)), ((), ()))
    grad_x_rows = lax.dot_general(
        combined, w_full, contract, preferred_element_type=jnp.float32
    ).astype(jnp.bfloat16)
    factor = 1.0 / math.sqrt(tok_count * seq_devices * dp_devices)
    over_tokens = (((0,), (0,)), ((), ()))
    term = (
        lax.dot_general(tokens, combined, over_tokens, preferred_element_type=jnp.float32) * factor
    ).astype(jnp.bfloat16)
    half = all_cols // 2
    core = dp_index % 2
    pairs = [(i, i ^ 1) for i in range(dp_devices)]
    keep = lax.dynamic_slice_in_dim(term, core * half, half, axis=1)
    give = lax.dynamic_slice_in_dim(term, (1 - core) * half, half, axis=1)
    got = lax.ppermute(give, "dp", pairs)
    chip_sum = (keep.astype(jnp.float32) + got.astype(jnp.float32)).astype(jnp.bfloat16)
    part = lax.psum_scatter(chip_sum, "seq", scatter_dimension=0, tiled=True)
    step = 2
    while step < dp_devices:
        mates = [(i, i ^ step) for i in range(dp_devices)]
        other = lax.ppermute(part, "dp", mates)
        part = (part.astype(jnp.float32) + other.astype(jnp.float32)).astype(jnp.bfloat16)
        step *= 2
    other_half = lax.ppermute(part, "dp", pairs)
    first = jnp.where(core == 0, part, other_half)
    second = jnp.where(core == 0, other_half, part)
    grad_all = jnp.concatenate([first, second], axis=1)
    grad_wq = grad_all[:, :query_cols]
    grad_wk = grad_all[:, query_cols : query_cols + kv_cols]
    grad_wv = grad_all[:, query_cols + kv_cols :]
    return (out_rows[None], grad_x_rows[None], grad_wq, grad_wk, grad_wv)


def solution(mesh):
    placed = (
        P("dp", "seq", None),
        P("seq", None),
        P("seq", None),
        P("seq", None),
        P(),
        P(),
        P("dp", "seq", None),
    )
    return jax.shard_map(
        per_device,
        mesh=mesh,
        in_specs=placed,
        out_specs=(
            P("dp", "seq", None),
            P("dp", "seq", None),
            P("seq", None),
            P("seq", None),
            P("seq", None),
        ),
        check_vma=False,
    )
```

profile of v0, /device:TPU:7, one launch (start us, length us, event | category | flops | bytes accessed | tf_op | source)
XLA Modules:
  0.0 728.5 jit_solution(3099953773682184216)
XLA Ops:
  7.2 1.8 pad_maximum_fusion.5
  10.4 112.5 %all-gather.2.cloned.1.call-done = bf16[2048,2560]{1,0:T(8,128)(2,1)} async-done(((bf16[64,2560]{1,0:T(8,128)(2,1)}), bf16[2048,2560]{1,0:T(8,128)(2,1)}) %all-gather.2.cloned.1.call-update) | async-done | bytes 10485776 | tf_op jit(solution)/shard_map/all_gather | solution.py:87
  122.8 6.9 fusion.43
  131.6 5.4 all-to-all-start
  139.2 46.5 %all-to-all-done = bf16[32,128,256]{1,2,0:T(8,128)(2,1)S(1)} async-done(((bf16[32,128,256]{1,2,0:T(8,128)(2,1)}), bf16[32,128,256]{1,2,0:T(8,128)(2,1)S(1)}, u32[]{:S(2)}, u32[]{:S(2)}) %all-to-all-start) | async-done | bytes 2097184 | tf_op jit(solution)/shard_map/all_to_all | solution.py:100
  185.7 2.9 copy.68
  188.6 4.2 fusion.53
  192.8 2.3 copy.72
  195.1 2.3 copy.71
  199.0 167.2 %while.15 = (s32[]{:T(128)}, f32[32,128,128]{2,1,0:T(8,128)}, bf16[8,4,128,64]{2,3,1,0:T(8,128)(2,1)}, bf16[8,4,128,64]{2,3,1,0:T(8,128)(2,1)}, s32[8,4,7]{2,1,0...) while((s32[]{:T(128)}, f32[32,128,128]{2,1,0:T(8,128)}, ...), condition=%wide.region_5.6_spmd.clone, body=%wide.region_0.5_spmd.clone.sunk | while | flops 360449568 | bytes 45045204 | solution.py:63
  199.3 1.7 gather_fusion.1
  201.7 1.6 fusion.93
  203.4 2.4 fusion.95
  211.4 1.7 copy.89
  213.1 6.9 scatter_fusion
  220.2 1.7 gather_fusion.1
  224.3 2.4 fusion.95
  232.3 1.7 copy.89
  234.0 6.9 scatter_fusion
  241.1 1.7 gather_fusion.1
  243.6 1.6 fusion.93
  245.2 2.4 fusion.95
  253.2 1.7 copy.89
  254.9 6.8 scatter_fusion
  262.0 1.7 gather_fusion.1
  264.4 1.6 fusion.93
  266.1 2.4 fusion.95
  274.1 1.7 copy.89
  275.8 6.8 scatter_fusion
  282.9 1.7 gather_fusion.1
  285.3 1.6 fusion.93
  287.0 2.4 fusion.95
  295.0 1.7 copy.89
  296.7 6.9 scatter_fusion
  303.8 1.7 gather_fusion.1
  306.3 1.6 fusion.93
  307.9 2.4 fusion.95
  315.9 1.7 copy.89
  317.6 6.8 scatter_fusion
  324.7 1.7 gather_fusion.1
  327.1 1.6 fusion.93
  328.8 2.4 fusion.95
  336.8 1.7 copy.89
  338.5 6.8 scatter_fusion
  345.6 1.7 gather_fusion.1
  348.0 1.6 fusion.93
  349.7 2.4 fusion.95
  357.7 1.7 copy.89
  359.4 6.8 scatter_fusion
  366.2 1.9 copy.73
  369.7 7.2 all-to-all-start.1
  377.1 49.0 %all-to-all-done.1 = bf16[32,128,256]{1,2,0:T(8,128)(2,1)S(1)} async-done(((bf16[32,128,256]{1,2,0:T(8,128)(2,1)}), bf16[32,128,256]{1,2,0:T(8,128)(2,1)S(1)}, u32[]{:S(2)}, u32[]{:S(2)}) %all-to-all-start.1) | async-done | bytes 2097184 | tf_op jit(solution)/shard_map/all_to_all | solution.py:118
  427.2 5.1 multiply_convert_fusion.1
  432.3 3.2 dynamic-slice_bitcast_fusion
  435.5 2.3 copy-done.1
  437.8 1.9 collective-permute-start
  439.7 8.6 %collective-permute-done = bf16[2048,1280]{0,1:T(8,128)(2,1)} collective-permute-done((bf16[2048,1280]{0,1:T(8,128)(2,1)}, bf16[2048,1280]{0,1:T(8,128)(2,1)}, u32[]{:S(2)}, u32[]{:S(2)}) %collective-permute-start) | collective-permute-done | bytes 5242912 | tf_op jit(solution)/shard_map/ppermute | solution.py:144
  448.3 9.4 %fusion.42 = bf16[2048,1280]{0,1:T(8,128)(2,1)} fusion(bf16[2048,1280]{0,1:T(8,128)(2,1)} %collective-permute-done, bf16[2560,2048]{1,0:T(8,128)(2,1)} %copy-done.1, s32[]{:T(128)S(6)} %select_n.59), kind=kLoop, calls=%fused_computation.54 | loop fusion | flops 10485760 | bytes 15728644 | tf_op jit(solution)/shard_map/convert_element_type | solution.py:145
  457.7 7.9 %copy.86 = bf16[2048,1280]{1,0:T(8,128)(2,1)} copy(bf16[2048,1280]{0,1:T(8,128)(2,1)} %fusion.42) | data formatting | bytes 10485760
  465.7 218.4 %reduce-scatter.4.cloned.1.call-done = bf16[64,1280]{1,0:T(8,128)(2,1)} async-done(((bf16[2048,1280]{1,0:T(8,128)(2,1)}), bf16[64,1280]{1,0:T(8,128)(2,1)}) %reduce-scatter.4.cloned.1.call-update) | async-done | bytes 163856
  685.5 5.7 collective-permute-done.1
  692.1 8.1 %collective-permute-done.2 = bf16[64,1280]{0,1:T(8,128)(2,1)S(1)} collective-permute-done((bf16[64,1280]{0,1:T(8,128)(2,1)S(1)}, bf16[64,1280]{0,1:T(8,128)(2,1)S(1)}, u32[]{:S(2)}, u32[]{:S(2)}) %collective-permute-start.2) | collective-permute-done | bytes 163872 | tf_op jit(solution)/shard_map/ppermute | solution.py:150
  700.4 9.5 %collective-permute-start.3 = (bf16[64,1280]{0,1:T(8,128)(2,1)S(1)}, bf16[64,1280]{0,1:T(8,128)(2,1)S(1)}, u32[]{:S(2)}, u32[]{:S(2)}) collective-permute-start(bf16[64,1280]{0,1:T(8,128)(2,1)S(1)} %add_convert_fusion), channel_id=1, source_target_pairs={{0,32},{32,0},{64,96},{96,64},{128,160},{160,128},{192,224},{224,1... | collective-permute-start | bytes 491528 | tf_op jit(solution)/shard_map/ppermute | solution.py:153
  709.9 8.3 %fusion.44 = bf16[1,128,2048]{2,1,0:T(8,128)(2,1)} fusion(bf16[2048,2560]{1,0:T(8,128)(2,1)} %all-gather.2.cloned.1.call-done, bf16[128,256]{0,1:T(8,128)(2,1)S(1)} %bitcast.151, bf16[128,256]{0,1:T(8,128)(2,1)S(1)} %bitcast.149, bf16[128,2048]{0,1:T(8,128)(2,1)S(1)} %bitcast.141), kind=kOutput, calls=%fused_computation.59 | convolution fusion | flops 1344405504 | bytes 11665408 | tf_op jit(solution)/shard_map/dot_general | solution.py:131
  (230 shorter events, 69.2 us)
Async XLA Ops:
  7.2 115.7 %copy-start = (bf16[1,128,2048]{2,1,0:T(8,128)(2,1)S(1)}, bf16[1,128,2048]{2,1,0:T(8,128)(2,1)}, u32[]{:S(2)}) copy-start(bf16[1,128,2048]{2,1,0:T(8,128)(2,1)} %param.9) | copy-start | bytes 1572868
  7.2 115.7 %all-gather.2.cloned.1.call-start = ((), (), s32[]{:S(2)}) async-start(), calls=%async_computation.3 | async-start | bytes 10813440 | tf_op jit(solution)/shard_map/all_gather | solution.py:87
  131.6 5.5 copy-start.10
  131.6 54.1 %all-to-all-start = ((bf16[32,128,256]{1,2,0:T(8,128)(2,1)}), bf16[32,128,256]{1,2,0:T(8,128)(2,1)S(1)}, u32[]{:S(2)}, u32[]{:S(2)}) async-start(bf16[32,128,256]{1,2,0:T(8,128)(2,1)} %pad_maximum_fusion.1), calls=%async_computation | async-start | bytes 4194304 | tf_op jit(solution)/shard_map/all_to_all | solution.py:100
  199.0 1.9 copy-start.2
  199.0 2.7 copy-start.4
  205.7 1.3 copy-start.6
  213.1 6.9 copy-start.3
  213.1 6.9 copy-start.5
  219.9 2.0 copy-start.2
  219.9 2.7 copy-start.4
  226.7 1.3 copy-start.6
  234.0 6.9 copy-start.3
  234.0 6.9 copy-start.5
  240.9 2.0 copy-start.2
  240.9 2.7 copy-start.4
  247.6 1.3 copy-start.6
  254.9 6.8 copy-start.3
  254.9 6.8 copy-start.5
  261.7 2.0 copy-start.2
  261.7 2.7 copy-start.4
  268.5 1.3 copy-start.6
  275.8 6.8 copy-start.3
  275.8 6.8 copy-start.5
  282.6 2.0 copy-start.2
  282.6 2.7 copy-start.4
  289.4 1.3 copy-start.6
  296.7 6.9 copy-start.3
  296.7 6.9 copy-start.5
  303.6 2.0 copy-start.2
  303.6 2.7 copy-start.4
  310.3 1.3 copy-start.6
  317.6 6.8 copy-start.3
  317.6 6.8 copy-start.5
  324.4 2.0 copy-start.2
  324.4 2.7 copy-start.4
  331.2 1.3 copy-start.6
  338.5 6.8 copy-start.3
  338.5 6.8 copy-start.5
  345.3 2.0 copy-start.2
  345.3 2.7 copy-start.4
  352.1 1.3 copy-start.6
  359.4 6.8 copy-start.3
  359.4 6.8 copy-start.5
  366.2 1.9 copy-start.8
  366.2 2.0 copy-start.9
  369.7 56.4 %all-to-all-start.1 = ((bf16[32,128,256]{1,2,0:T(8,128)(2,1)}), bf16[32,128,256]{1,2,0:T(8,128)(2,1)S(1)}, u32[]{:S(2)}, u32[]{:S(2)}) async-start(bf16[32,128,256]{1,2,0:T(8,128)(2,1)} %pad_maximum_fusion.2), calls=%async_computation.1 | async-start | bytes 4194304 | tf_op jit(solution)/shard_map/all_to_all | solution.py:118
  376.9 307.2 %reduce-scatter.4.cloned.1.call-start = ((), (), s32[]{:S(2)}) async-start(), calls=%async_computation.4 | async-start | bytes 5406720
  432.3 5.5 copy-start.1
  437.8 10.6 %collective-permute-start = (bf16[2048,1280]{0,1:T(8,128)(2,1)}, bf16[2048,1280]{0,1:T(8,128)(2,1)}, u32[]{:S(2)}, u32[]{:S(2)}) collective-permute-start(bf16[2048,1280]{0,1:T(8,128)(2,1)} %dynamic-slice_bitcast_fusion), channel_id=1, source_target_pairs={{0,32},{32,0},{64,96},{96,64},{128,160},{160,128},{192,224},{224,1... | collective-permute-start | bytes 15728648 | tf_op jit(solution)/shard_map/ppermute | solution.py:144
  685.2 6.0 collective-permute-start.1
  691.3 9.0 %collective-permute-start.2 = (bf16[64,1280]{0,1:T(8,128)(2,1)S(1)}, bf16[64,1280]{0,1:T(8,128)(2,1)S(1)}, u32[]{:S(2)}, u32[]{:S(2)}) collective-permute-start(bf16[64,1280]{0,1:T(8,128)(2,1)S(1)} %add_convert_fusion.1), channel_id=1, source_target_pairs={{0,128},{32,160},{64,192},{96,224},{128,0},{160,32},{192,64},{224,... | collective-permute-start | bytes 491528 | tf_op jit(solution)/shard_map/ppermute | solution.py:150
  700.4 17.8 %copy-start.7 = (bf16[32,128,64]{1,2,0:T(8,128)(2,1)S(1)}, bf16[32,128,64]{1,2,0:T(8,128)(2,1)}, u32[]{:S(2)}) copy-start(bf16[32,128,64]{1,2,0:T(8,128)(2,1)} %get-tuple-element.162) | copy-start | bytes 1572868
  700.4 18.8 %collective-permute-start.3 = (bf16[64,1280]{0,1:T(8,128)(2,1)S(1)}, bf16[64,1280]{0,1:T(8,128)(2,1)S(1)}, u32[]{:S(2)}, u32[]{:S(2)}) collective-permute-start(bf16[64,1280]{0,1:T(8,128)(2,1)S(1)} %add_convert_fusion), channel_id=1, source_target_pairs={{0,32},{32,0},{64,96},{96,64},{128,160},{160,128},{192,224},{224,1... | collective-permute-start | bytes 491528 | tf_op jit(solution)/shard_map/ppermute | solution.py:153
Sparse Core Ops, SparseCore 0:
  11.2 111.6 all-gather.1
  465.8 218.2 reduce-scatter.3
where the time goes:
time: 731 us; the launch traced here: 729 us
  waiting for transfers between devices  449 us (61%)
  matrix products  93.4 us (13%)
  other arithmetic  73.4 us (10%)
  local copies, waits for them, and re-layouts  72 us (10%)
  starting transfers between devices  25.4 us (3%)
  between operations  14.9 us (2%)
    unnamed x3, waiting for transfers between devices  218 us
    all_gather x1, waiting for transfers between devices, per_device(): w_full = lax.all_gather(w_local, 'seq', axis=0, tiled=True)  112 us
    scatter-add x8, other arithmetic, one_step(): running = running.at[chosen.reshape(-1)].add(pieces)  54.7 us
    all_to_all x1, waiting for transfers between devices, per_device(): lax.all_to_all(back_sent, 'seq', split_axis=0, concat_axis=0, tiled=True)  49 us
    all_to_all x1, waiting for transfers between devices, per_device(): lax.all_to_all(sent, 'seq', split_axis=0, concat_axis=1, tiled=True)[0]  46.5 us
    unnamed x21, local copies, waits for them, and re-layouts  20.6 us
    dot_general x8, matrix products, one_step(): jnp.einsum('gqk,gke->gqe', shares_low, v_part, preferred_element_type=jnp...  19.1 us
  transfers between devices with their start and end apart: 8, of which 7 were waited for; matrix products, arithmetic and copies ran while one was open for 2% of the time, Pallas kernels for 0%

commit v1 on v0

--- a/solution.py
+++ b/solution.py
@@ -97,7 +97,10 @@
     )
     kv_pieces = jnp.repeat(paired.transpose(1, 0, 2), GROUP, axis=0)
     sent = jnp.concatenate([query_pieces, grad_pieces, kv_pieces], axis=2)
-    landed = lax.all_to_all(sent, "seq", split_axis=0, concat_axis=1, tiled=True)[0]
+    landed = jnp.concatenate(
+        lax.all_to_all(jnp.stack(jnp.split(sent, lax.axis_size("seq"), axis=0)), "seq", 0, 0),
+        axis=1,
+    )[0]
     head_q = landed[:, :HD]
     head_grad = landed[:, HD : 2 * HD]
     head_k = landed[:, 2 * HD : 3 * HD]

time: 731 us -> 736 us (level)
  local copies, waits for them, and re-layouts: 72 us -> 105 us
  matrix products: 93.4 us -> 65.7 us
    unnamed x21 -> x52, local copies, waits for them, and re-layouts: 20.6 us -> 36.6 us
    dynamic_slice x0 -> x8, local copies, waits for them, and re-layouts: none -> 7.78 us  [head_pass(): lax.scan(one_step, initial, (query_steps, grad_steps, block_steps))]
    dot_general x8, matrix products: 10.3 us -> 2.97 us  [one_step(): jnp.einsum('gqk,gqe->gke', shares_low, g_part, preferred_element_type=jnp...]
where the time goes in v1:
time: 736 us; the launch traced here: 734 us
  waiting for transfers between devices  446 us (61%)
  local copies, waits for them, and re-layouts  105 us (14%)
  other arithmetic  74 us (10%)
  matrix products  65.7 us (9%)
  starting transfers between devices  27.2 us (4%)
  between operations  15 us (2%)
    unnamed x3, waiting for transfers between devices  218 us
    all_gather x1, waiting for transfers between devices, per_device(): w_full = lax.all_gather(w_local, 'seq', axis=0, tiled=True)  112 us
    scatter-add x8, other arithmetic, one_step(): running = running.at[chosen.reshape(-1)].add(pieces)  55.9 us
    all_to_all x1, waiting for transfers between devices, per_device(): lax.all_to_all(back_sent, 'seq', split_axis=0, concat_axis=0, tiled=True)  48.6 us
    all_to_all x1, waiting for transfers between devices, per_device(): lax.all_to_all(jnp.stack(jnp.split(sent, lax.axis_size('seq'), axis=0)),...  46.3 us
    unnamed x52, local copies, waits for them, and re-layouts  36.6 us
    dot_general x8, matrix products, one_step(): jnp.einsum('gqk,gke->gqe', shares_low, v_part, preferred_element_type=jnp...  19.1 us
  transfers between devices with their start and end apart: 8, of which 7 were waited for; matrix products, arithmetic and copies ran while one was open for 2% of the time, Pallas kernels for 0%

profile of v1, /device:TPU:7, one launch (start us, length us, event | category | flops | bytes accessed | tf_op | source)
XLA Modules:
  0.0 734.0 jit_solution(5973791993855364121)
XLA Ops:
  7.2 1.8 pad_maximum_fusion.5
  9.0 1.3 copy.130
  10.9 112.0 %all-gather.2.cloned.1.call-done = bf16[2048,2560]{1,0:T(8,128)(2,1)} async-done(((bf16[64,2560]{1,0:T(8,128)(2,1)}), bf16[2048,2560]{1,0:T(8,128)(2,1)}) %all-gather.2.cloned.1.call-update) | async-done | bytes 10485776 | tf_op jit(solution)/shard_map/all_gather | solution.py:87
  122.8 6.9 fusion.23
  151.7 5.6 all-to-all-start
  159.5 46.3 %all-to-all-done = bf16[32,1,128,256]{3,2,1,0:T(8,128)(2,1)S(1)} async-done(((bf16[32,1,128,256]{3,2,1,0:T(8,128)(2,1)}), bf16[32,1,128,256]{3,2,1,0:T(8,128)(2,1)S(1)}, u32[]{:S(2)}, u32[]{:S(2)}) %all-to-all-start) | async-done | bytes 2097184 | tf_op jit(solution)/shard_map/all_to_all | solution.py:101
  205.8 1.3 copy-done.7
  207.1 4.2 fusion.31
  211.3 1.6 copy.152
  212.9 2.3 copy.154
  215.2 1.6 broadcast_in_dim.33
  216.8 155.2 %while.15 = (s32[]{:T(128)}, f32[32,128,128]{2,1,0:T(8,128)}, bf16[8,4,128,64]{2,3,1,0:T(8,128)(2,1)}, bf16[8,4,128,64]{2,3,1,0:T(8,128)(2,1)}, s32[8,4,7]{2,1,0...) while((s32[]{:T(128)}, f32[32,128,128]{2,1,0:T(8,128)}, ...), condition=%wide.region_5.6_spmd.clone, body=%wide.region_0.5_spmd.clone.sunk | while | flops 360449568 | bytes 49501696 | solution.py:63
  218.0 1.7 gather_fusion.1
  221.2 2.4 fusion.67
  225.8 1.2 fusion.68
  227.4 1.7 copy.179
  229.1 7.0 scatter_fusion
  237.4 1.7 gather_fusion.1
  240.6 2.4 fusion.67
  246.8 1.7 copy.179
  248.5 7.0 scatter_fusion
  256.9 1.7 gather_fusion.1
  260.1 2.4 fusion.67
  266.3 1.7 copy.179
  268.0 7.0 scatter_fusion
  276.2 1.7 gather_fusion.1
  279.5 2.4 fusion.67
  285.7 1.7 copy.179
  287.4 7.0 scatter_fusion
  295.7 1.7 gather_fusion.1
  298.9 2.4 fusion.67
  305.1 1.7 copy.179
  306.8 7.0 scatter_fusion
  315.0 1.7 gather_fusion.1
  318.3 2.4 fusion.67
  322.9 1.2 fusion.68
  324.5 1.7 copy.179
  326.2 6.9 scatter_fusion
  334.4 1.7 gather_fusion.1
  337.6 2.4 fusion.67
  342.2 1.2 fusion.68
  343.8 1.7 copy.179
  345.5 7.0 scatter_fusion
  353.8 1.7 gather_fusion.1
  357.1 2.4 fusion.67
  363.3 1.7 copy.179
  365.0 7.0 scatter_fusion
  372.0 1.9 copy.137
  374.0 1.5 pad_maximum_fusion.2
  375.5 7.1 all-to-all-start.1
  382.6 48.6 %all-to-all-done.1 = bf16[32,128,256]{1,2,0:T(8,128)(2,1)S(1)} async-done(((bf16[32,128,256]{1,2,0:T(8,128)(2,1)}), bf16[32,128,256]{1,2,0:T(8,128)(2,1)S(1)}, u32[]{:S(2)}, u32[]{:S(2)}) %all-to-all-start.1) | async-done | bytes 2097184 | tf_op jit(solution)/shard_map/all_to_all | solution.py:121
  432.3 5.1 multiply_convert_fusion.1
  437.4 3.3 dynamic-slice_bitcast_fusion
  440.7 2.3 copy-done.1
  442.9 2.5 collective-permute-start
  445.4 8.6 %collective-permute-done = bf16[2048,1280]{0,1:T(8,128)(2,1)} collective-permute-done((bf16[2048,1280]{0,1:T(8,128)(2,1)}, bf16[2048,1280]{0,1:T(8,128)(2,1)}, u32[]{:S(2)}, u32[]{:S(2)}) %collective-permute-start) | collective-permute-done | bytes 5242912 | tf_op jit(solution)/shard_map/ppermute | solution.py:147
  454.0 9.5 %fusion.22 = bf16[2048,1280]{0,1:T(8,128)(2,1)} fusion(bf16[2048,1280]{0,1:T(8,128)(2,1)} %collective-permute-done, bf16[2560,2048]{1,0:T(8,128)(2,1)} %copy-done.1, s32[]{:T(128)S(6)} %select_n.59), kind=kLoop, calls=%fused_computation.43 | loop fusion | flops 10485760 | bytes 15728644 | tf_op jit(solution)/shard_map/convert_element_type | solution.py:148
  463.5 7.8 %copy.146 = bf16[2048,1280]{1,0:T(8,128)(2,1)} copy(bf16[2048,1280]{0,1:T(8,128)(2,1)} %fusion.22) | data formatting | bytes 10485760
  471.3 218.0 %reduce-scatter.4.cloned.1.call-done = bf16[64,1280]{1,0:T(8,128)(2,1)} async-done(((bf16[2048,1280]{1,0:T(8,128)(2,1)}), bf16[64,1280]{1,0:T(8,128)(2,1)}) %reduce-scatter.4.cloned.1.call-update) | async-done | bytes 163856
  691.6 5.0 collective-permute-done.1
  696.6 1.7 collective-permute-start.2
  698.3 7.7 %collective-permute-done.2 = bf16[64,1280]{0,1:T(8,128)(2,1)S(1)} collective-permute-done((bf16[64,1280]{0,1:T(8,128)(2,1)S(1)}, bf16[64,1280]{0,1:T(8,128)(2,1)S(1)}, u32[]{:S(2)}, u32[]{:S(2)}) %collective-permute-start.2) | collective-permute-done | bytes 163872 | tf_op jit(solution)/shard_map/ppermute | solution.py:153
  706.2 9.2 %collective-permute-start.3 = (bf16[64,1280]{0,1:T(8,128)(2,1)S(1)}, bf16[64,1280]{0,1:T(8,128)(2,1)S(1)}, u32[]{:S(2)}, u32[]{:S(2)}) collective-permute-start(bf16[64,1280]{0,1:T(8,128)(2,1)S(1)} %add_convert_fusion), channel_id=1, source_target_pairs={{0,32},{32,0},{64,96},{96,64},{128,160},{160,128},{192,224},{224,1... | collective-permute-start | bytes 491528 | tf_op jit(solution)/shard_map/ppermute | solution.py:156
  715.4 8.3 %fusion.24 = bf16[1,128,2048]{2,1,0:T(8,128)(2,1)} fusion(bf16[2048,2560]{1,0:T(8,128)(2,1)} %all-gather.2.cloned.1.call-done, bf16[128,256]{0,1:T(8,128)(2,1)S(1)} %bitcast.276, bf16[128,256]{0,1:T(8,128)(2,1)S(1)} %bitcast.274, bf16[128,2048]{0,1:T(8,128)(2,1)S(1)} %bitcast.265), kind=kOutput, calls=%fused_computation.48 | convolution fusion | flops 1344405504 | bytes 11665408 | tf_op jit(solution)/shard_map/dot_general | solution.py:134
  (306 shorter events, 79.6 us)
Async XLA Ops:
  7.2 115.7 %copy-start = (bf16[1,128,2048]{2,1,0:T(8,128)(2,1)S(1)}, bf16[1,128,2048]{2,1,0:T(8,128)(2,1)}, u32[]{:S(2)}) copy-start(bf16[1,128,2048]{2,1,0:T(8,128)(2,1)} %param.9) | copy-start | bytes 1572868
  7.2 115.7 %all-gather.2.cloned.1.call-start = ((), (), s32[]{:S(2)}) async-start(), calls=%async_computation.3 | async-start | bytes 10813440 | tf_op jit(solution)/shard_map/all_gather | solution.py:87
  151.7 5.7 copy-start.13
  151.7 54.1 %all-to-all-start = ((bf16[32,1,128,256]{3,2,1,0:T(8,128)(2,1)}), bf16[32,1,128,256]{3,2,1,0:T(8,128)(2,1)S(1)}, u32[]{:S(2)}, u32[]{:S(2)}) async-start(bf16[32,1,128,256]{3,2,1,0:T(8,128)(2,1)} %constant_dynamic-update-slice_fusion), calls=%async_computation | async-start | bytes 4194304 | tf_op jit(solution)/shard_map/all_to_all | solution.py:101
  205.8 1.3 copy-start.7
  216.8 2.9 copy-start.2
  216.8 3.7 copy-start.4
  216.8 3.7 copy-start.9
  223.6 1.2 copy-start.6
  229.1 7.0 copy-start.3
  229.1 7.0 copy-start.5
  229.1 7.0 copy-start.10
  236.1 3.0 copy-start.2
  236.1 3.7 copy-start.4
  236.2 3.7 copy-start.9
  248.5 7.0 copy-start.3
  248.5 7.0 copy-start.5
  248.5 7.0 copy-start.10
  255.6 3.0 copy-start.2
  255.6 3.7 copy-start.4
  255.6 3.7 copy-start.9
  268.0 7.0 copy-start.3
  268.0 7.0 copy-start.5
  268.0 7.0 copy-start.10
  275.0 3.0 copy-start.2
  275.0 3.7 copy-start.4
  275.0 3.7 copy-start.9
  287.4 7.0 copy-start.3
  287.4 7.0 copy-start.5
  287.4 7.0 copy-start.10
  294.4 3.0 copy-start.2
  294.4 3.7 copy-start.4
  294.4 3.7 copy-start.9
  306.8 7.0 copy-start.3
  306.8 7.0 copy-start.5
  306.8 7.0 copy-start.10
  313.8 3.0 copy-start.2
  313.8 3.7 copy-start.4
  313.8 3.7 copy-start.9
  326.2 6.9 copy-start.3
  326.2 6.9 copy-start.5
  326.2 6.9 copy-start.10
  333.1 3.0 copy-start.2
  333.1 3.7 copy-start.4
  333.2 3.7 copy-start.9
  345.5 7.0 copy-start.3
  345.5 7.0 copy-start.5
  345.5 7.0 copy-start.10
  352.6 3.0 copy-start.2
  352.6 3.7 copy-start.4
  352.6 3.7 copy-start.9
  365.0 7.0 copy-start.3
  365.0 7.0 copy-start.5
  365.0 7.0 copy-start.10
  372.0 2.0 copy-start.11
  372.0 2.0 copy-start.12
  375.5 55.8 %all-to-all-start.1 = ((bf16[32,128,256]{1,2,0:T(8,128)(2,1)}), bf16[32,128,256]{1,2,0:T(8,128)(2,1)S(1)}, u32[]{:S(2)}, u32[]{:S(2)}) async-start(bf16[32,128,256]{1,2,0:T(8,128)(2,1)} %pad_maximum_fusion.2), calls=%async_computation.1 | async-start | bytes 4194304 | tf_op jit(solution)/shard_map/all_to_all | solution.py:121
  382.6 306.8 %reduce-scatter.4.cloned.1.call-start = ((), (), s32[]{:S(2)}) async-start(), calls=%async_computation.4 | async-start | bytes 5406720
  437.4 5.6 copy-start.1
  442.9 11.1 %collective-permute-start = (bf16[2048,1280]{0,1:T(8,128)(2,1)}, bf16[2048,1280]{0,1:T(8,128)(2,1)}, u32[]{:S(2)}, u32[]{:S(2)}) collective-permute-start(bf16[2048,1280]{0,1:T(8,128)(2,1)} %dynamic-slice_bitcast_fusion), channel_id=1, source_target_pairs={{0,32},{32,0},{64,96},{96,64},{128,160},{160,128},{192,224},{224,1... | collective-permute-start | bytes 15728648 | tf_op jit(solution)/shard_map/ppermute | solution.py:147
  690.5 6.0 collective-permute-start.1
  696.6 9.4 %collective-permute-start.2 = (bf16[64,1280]{0,1:T(8,128)(2,1)S(1)}, bf16[64,1280]{0,1:T(8,128)(2,1)S(1)}, u32[]{:S(2)}, u32[]{:S(2)}) collective-permute-start(bf16[64,1280]{0,1:T(8,128)(2,1)S(1)} %add_convert_fusion.1), channel_id=1, source_target_pairs={{0,128},{32,160},{64,192},{96,224},{128,0},{160,32},{192,64},{224,... | collective-permute-start | bytes 491528 | tf_op jit(solution)/shard_map/ppermute | solution.py:153
  706.1 17.5 %copy-start.8 = (bf16[32,128,64]{1,2,0:T(8,128)(2,1)S(1)}, bf16[32,128,64]{1,2,0:T(8,128)(2,1)}, u32[]{:S(2)}) copy-start(bf16[32,128,64]{1,2,0:T(8,128)(2,1)} %get-tuple-element.164) | copy-start | bytes 1572868
  706.2 18.5 %collective-permute-start.3 = (bf16[64,1280]{0,1:T(8,128)(2,1)S(1)}, bf16[64,1280]{0,1:T(8,128)(2,1)S(1)}, u32[]{:S(2)}, u32[]{:S(2)}) collective-permute-start(bf16[64,1280]{0,1:T(8,128)(2,1)S(1)} %add_convert_fusion), channel_id=1, source_target_pairs={{0,32},{32,0},{64,96},{96,64},{128,160},{160,128},{192,224},{224,1... | collective-permute-start | bytes 491528 | tf_op jit(solution)/shard_map/ppermute | solution.py:156
  (7 other events, 8.3 us)
Sparse Core Ops, SparseCore 0:
  11.2 111.6 all-gather.1
  471.5 217.8 reduce-scatter.3
